TPU v7x, 512 devices: a whole 4x8x8 slice. The times are simulated.
512 devices in a mesh: dp: 16 (over z_hi, y), tensor: 32 (over x, z_lo, core).
Axes of the slice: x: 4, y: 8, z: 8 (z_hi: 2, z_lo: 4; z = z_hi * 4 + z_lo), core: 2. Of those that a mesh axis runs over, the one named last changes fastest.
Arguments:
- suffix_states: bfloat16 [32, 128, 2048], P(None, 'dp', 'tensor'), may hold values from -16 to 16
- suffix_lengths: int32 [32], replicated, may hold values from 1 to 128, 2560 in all
- request_group: int32 [32, 1], replicated, may hold values from 0 to 15
- group_owner: int32 [16], replicated, may hold values from 0 to 15, each once
- request_order: int32 [32], replicated, may hold values from 0 to 31, each once
- prefix_cache: bfloat16 [16, 256, 1024], P('dp', 'tensor'), may hold values from -700 to 700
- norm_attn: bfloat16 [2048], replicated, may hold values from 0.099609375 to 1.8984375
- w_query: bfloat16 [2048, 2048], P(None, 'tensor'), may hold values from -0.125 to 0.125
- w_key: bfloat16 [2048, 512], P(None, 'tensor'), may hold values from -0.125 to 0.125
- w_value: bfloat16 [2048, 512], P(None, 'tensor'), may hold values from -0.125 to 0.125
- w_out: bfloat16 [2048, 2048], P('tensor'), may hold values from -0.25 to 0.25
- norm_mlp: bfloat16 [2048], replicated, may hold values from 0.099609375 to 1.8984375
- w_gate: bfloat16 [2048, 8192], P(None, 'tensor'), may hold values from -0.125 to 0.125
- w_up: bfloat16 [2048, 8192], P(None, 'tensor'), may hold values from -0.125 to 0.125
- w_down: bfloat16 [8192, 2048], P('tensor'), may hold values from -0.125 to 0.125
Outputs:
- hidden_out: bfloat16 [32, 128, 2048], P(None, 'dp', 'tensor')
- suffix_keys: bfloat16 [32, 128, 512], P('dp', None, 'tensor')
- suffix_values: bfloat16 [32, 128, 512], P('dp', None, 'tensor')
Inputs may be any that keep to these rules, and one draw needn't show every extreme that they name: `suffix_lengths`: the lengths sum to 2560 and some request has exactly 128. `request_group`: every group has at least one request. `group_owner`: A permutation of the 16 groups onto the slots of prefix_cache. `request_order`: A permutation of the requests; slot s belongs to index s // 2 of dp.
All inputs are finite; a program needn't handle non-finite values.
Results may differ from a plain program's by a relative error of at most 0.03.
Values may be sent and summed in bfloat16 or wider, within the bound.
No kernel may reach another device: no remote copies, remote signals or barrier semaphores. Data moves between devices by JAX's collectives and lax.ppermute only.
A program may use at most 64 MiB of HBM per device.

v0:
```python
import jax
import jax.numpy as jnp
import numpy as np
from jax import lax
from jax.sharding import PartitionSpec as P

H = 32
KVH = 8
HD = 64
L_MAX = 128
P_SIZE = 256
THETA = 10000000.0
EPSILON = 1e-05


def rms_scale(wide, gain):
    mean_square = jnp.mean(wide * wide, axis=-1, keepdims=True)
    return (wide * lax.rsqrt(mean_square + EPSILON) * gain.astype(jnp.float32)).astype(jnp.bfloat16)


def rotate(vectors, positions):
    half = HD // 2
    freqs = THETA ** (-(jnp.arange(half, dtype=jnp.float32) * 2.0 / HD))
    angles = positions[:, None] * freqs[None, :]
    cosine = jnp.cos(angles)
    sine = jnp.sin(angles)
    first = vectors[..., :half]
    second = vectors[..., half:]
    return jnp.concatenate(
        [first * cosine - second * sine, second * cosine + first * sine], axis=-1
    )


def gather_rows(shard, axis_name, count):
    sent = jnp.broadcast_to(shard[None], (count,) + shard.shape)
    got = lax.all_to_all(sent, axis_name, 0, 0, tiled=True)
    rows, width = shard.shape
    return got.transpose(1, 0, 2).reshape(rows, count * width)


def scatter_sum(terms, axis_name, count):
    rows, width = terms.shape
    share = width // count
    sent = terms.astype(jnp.bfloat16).reshape(rows, count, share).transpose(1, 0, 2)
    got = lax.all_to_all(sent, axis_name, 0, 0, tiled=True)
    return jnp.sum(got.astype(jnp.float32), axis=0)


def shards(
    suffix_states,
    suffix_lengths,
    request_group,
    group_owner,
    request_order,
    prefix_cache,
    norm_attn,
    w_query,
    w_key,
    w_value,
    w_out,
    norm_mlp,
    w_gate,
    w_up,
    w_down,
):
    dp_count = lax.axis_size("dp")
    tp_count = lax.axis_size("tensor")
    dp_index = lax.axis_index("dp")
    tp_index = lax.axis_index("tensor")
    total_reqs = suffix_lengths.shape[0]
    local_reqs = total_reqs // dp_count
    row_count = local_reqs * L_MAX
    heads_here = w_query.shape[1] // HD
    group_size = H // KVH
    assert heads_here == 1
    kv_cols = w_key.shape[1]
    d_here = kv_cols // KVH
    score_scale = HD ** (-0.5)
    kv_of_dest = np.arange(tp_count) * heads_here // group_size
    kv_here = tp_index * heads_here // group_size
    col_pick = (np.arange(d_here)[None, :] * KVH + kv_of_dest[:, None]).reshape(-1)
    w_pair = jnp.concatenate([w_key, w_value], axis=1)
    pick = np.concatenate(
        [col_pick.reshape(tp_count, d_here), kv_cols + col_pick.reshape(tp_count, d_here)], axis=1
    )
    w_sent = jnp.take(w_pair, pick.reshape(-1), axis=1).reshape(
        w_key.shape[0], tp_count, 2 * d_here
    )
    w_sent = w_sent.transpose(1, 0, 2).reshape(tp_count, -1)
    routed = jnp.take(suffix_states, request_order, axis=0)
    pos_here = routed.shape[1]
    width_here = routed.shape[2]
    state_part = routed.reshape(dp_count, local_reqs * pos_here * width_here)
    prefix_flat = prefix_cache.reshape(1, -1)
    prefix_part = jnp.broadcast_to(prefix_flat, (dp_count, prefix_flat.shape[1]))
    first = lax.all_to_all(
        jnp.concatenate([state_part, prefix_part], axis=1), "dp", 0, 0, tiled=True
    )
    state_split = state_part.shape[1]
    routed_here = (
        first[:, :state_split]
        .reshape(dp_count, local_reqs, pos_here, width_here)
        .transpose(1, 0, 2, 3)
        .reshape(local_reqs, dp_count * pos_here, width_here)
    )
    prefix_rows = prefix_cache.shape[1]
    prefix_all = first[:, state_split:].reshape(dp_count, prefix_rows, KVH, 2 * HD)
    state_shard = routed_here.reshape(row_count, width_here)
    slot_ids = dp_index * local_reqs + jnp.arange(local_reqs, dtype=jnp.int32)
    req_ids = jnp.take(request_order, slot_ids)
    lengths_here = jnp.take(suffix_lengths, req_ids)
    owner_here = jnp.take(group_owner, jnp.take(request_group[:, 0], req_ids))
    position = jnp.arange(L_MAX, dtype=jnp.int32)
    valid = (position[None, :] < lengths_here[:, None]).reshape(row_count)
    positions = (P_SIZE + position).astype(jnp.float32)
    chosen = jnp.take(prefix_all, owner_here, axis=0)
    chosen = jnp.take(chosen, kv_of_dest, axis=2).transpose(2, 0, 1, 3)
    state_sent = jnp.broadcast_to(state_shard.reshape(1, -1), (tp_count, row_count * width_here))
    prefix_sent = chosen.reshape(tp_count, -1)
    cuts = np.cumsum([state_sent.shape[1], prefix_sent.shape[1]])
    got = lax.all_to_all(
        jnp.concatenate([state_sent, prefix_sent, w_sent], axis=1), "tensor", 0, 0, tiled=True
    )
    full_rows = (
        got[:, : cuts[0]]
        .reshape(tp_count, row_count, width_here)
        .transpose(1, 0, 2)
        .reshape(row_count, tp_count * width_here)
    )
    picked = got[:, cuts[0] : cuts[1]].reshape(tp_count, local_reqs, prefix_rows, 2 * HD)
    picked = picked.transpose(1, 0, 2, 3).reshape(local_reqs, tp_count * prefix_rows, 2 * HD)
    prefix_keys = picked[:, :, :HD]
    prefix_values = picked[:, :, HD:]
    w_got = got[:, cuts[1] :].reshape(tp_count, w_key.shape[0], 2 * d_here)
    k_head_w = w_got[:, :, :d_here].transpose(1, 0, 2).reshape(w_key.shape[0], HD)
    v_head_w = w_got[:, :, d_here:].transpose(1, 0, 2).reshape(w_key.shape[0], HD)
    normed = rms_scale(full_rows.astype(jnp.float32), norm_attn)
    query = jnp.dot(normed, w_query, preferred_element_type=jnp.float32).reshape(
        local_reqs, L_MAX, HD
    )
    query = rotate(query, positions).astype(jnp.bfloat16)
    key_raw = jnp.dot(normed, k_head_w, preferred_element_type=jnp.float32).astype(jnp.bfloat16)
    value = jnp.dot(normed, v_head_w, preferred_element_type=jnp.float32).astype(jnp.bfloat16)
    key_rot = rotate(key_raw.reshape(local_reqs, L_MAX, HD).astype(jnp.float32), positions).astype(
        jnp.bfloat16
    )
    value = value.reshape(local_reqs, L_MAX, HD)
    valid3 = valid.reshape(local_reqs, L_MAX, 1)
    out_width = kv_cols
    out_first = tp_index * out_width % HD
    keys_out = jnp.where(
        valid3, lax.dynamic_slice_in_dim(key_rot, out_first, out_width, 2), 0.0
    ).astype(jnp.bfloat16)
    values_out = jnp.where(
        valid3, lax.dynamic_slice_in_dim(value, out_first, out_width, 2), 0.0
    ).astype(jnp.bfloat16)
    prefix_scores = (
        jnp.einsum("rtd,rpd->rtp", query, prefix_keys, preferred_element_type=jnp.float32)
        * score_scale
    )
    self_scores = (
        jnp.einsum("rtd,rsd->rts", query, key_rot, preferred_element_type=jnp.float32) * score_scale
    )
    self_allowed = (position[None, None, :] <= position[None, :, None]) & (
        position[None, None, :] < lengths_here[:, None, None]
    )
    scores = jnp.concatenate([prefix_scores, self_scores], axis=2)
    allowed = jnp.concatenate([jnp.ones(prefix_scores.shape, bool), self_allowed], axis=2)
    row_peak = jnp.max(jnp.where(allowed, scores, -jnp.inf), axis=2, keepdims=True)
    weights = jnp.where(allowed, jnp.exp(scores - row_peak), 0.0)
    total = jnp.sum(weights, axis=2, keepdims=True)
    all_values = jnp.concatenate([prefix_values, value], axis=1)
    numerator = jnp.einsum(
        "rtk,rkd->rtd", weights.astype(jnp.bfloat16), all_values, preferred_element_type=jnp.float32
    )
    attention = (numerator / total).astype(jnp.bfloat16).reshape(row_count, HD)
    attn_terms = jnp.dot(attention, w_out, preferred_element_type=jnp.float32)
    attn_share = scatter_sum(attn_terms, "tensor", tp_count)
    middle = (state_shard.astype(jnp.float32) + attn_share).astype(jnp.bfloat16)
    middle_rows = gather_rows(middle, "tensor", tp_count)
    normed_two = rms_scale(middle_rows.astype(jnp.float32), norm_mlp)
    gate = jnp.dot(normed_two, w_gate, preferred_element_type=jnp.float32)
    upper = jnp.dot(normed_two, w_up, preferred_element_type=jnp.float32)
    hidden = (jax.nn.silu(gate) * upper).astype(jnp.bfloat16)
    down_terms = jnp.dot(hidden, w_down, preferred_element_type=jnp.float32)
    down_share = scatter_sum(down_terms, "tensor", tp_count)
    result = middle.astype(jnp.float32) + down_share
    result = (
        jnp.where(valid[:, None], result, 0.0)
        .astype(jnp.bfloat16)
        .reshape(local_reqs, L_MAX, width_here)
    )
    returned = lax.all_to_all(result, "dp", split_axis=1, concat_axis=0, tiled=True)
    hidden_out = jnp.zeros_like(returned).at[request_order].set(returned)
    return (hidden_out, keys_out, values_out)


def solution(mesh):
    in_specs = (
        P(None, "dp", "tensor"),
        P(),
        P(),
        P(),
        P(),
        P("dp", "tensor", None),
        P(),
        P(None, "tensor"),
        P(None, "tensor"),
        P(None, "tensor"),
        P("tensor", None),
        P(),
        P(None, "tensor"),
        P(None, "tensor"),
        P("tensor", None),
    )
    out_specs = (P(None, "dp", "tensor"), P("dp", None, "tensor"), P("dp", None, "tensor"))
    return jax.shard_map(shards, mesh=mesh, in_specs=in_specs, out_specs=out_specs, check_vma=False)
```

profile of v0, /device:TPU:1, one launch (start us, length us, event | category | flops | bytes accessed | tf_op | source)
XLA Modules:
  0.0 274.5 jit_solution(12985198102943313836)
XLA Ops:
  6.9 16.2 %all-to-all-start = ((bf16[16,2,4608]{2,1,0:T(2,128)(2,1)}), bf16[16,2,4608]{2,1,0:T(2,128)(2,1)}, u32[]{:S(2)}, u32[]{:S(2)}) async-start(bf16[16,2,4608]{2,1,0:T(2,128)(2,1)} %reshape.434), calls=%async_computation | async-start | bytes 589824 | tf_op jit(solution)/shard_map/all_to_all | solution.py:96
  27.1 3.1 %copy.162 = bf16[2048,32,4]{1,2,0:T(4,128)(2,1)S(1)} copy(bf16[2048,32,4]{0,2,1:T(4,128)(2,1)} %gather.30) | data formatting | bytes 1048576 | tf_op jit(solution)/shard_map/jit(_take)/gather | solution.py:86
  32.5 4.2 %all-to-all-done = bf16[16,2,4608]{2,1,0:T(2,128)(2,1)} async-done(((bf16[16,2,4608]{2,1,0:T(2,128)(2,1)}), bf16[16,2,4608]{2,1,0:T(2,128)(2,1)}, u32[]{:S(2)}, u32[]{:S(2)}) %all-to-all-start) | async-done | bytes 294944 | tf_op jit(solution)/shard_map/all_to_all | solution.py:96
  36.6 2.2 reshape.435
  40.8 2.6 reduce.5
  43.5 3.4 %reshape.436 = bf16[32,2,13312]{2,1,0:T(2,128)(2,1)} reshape(bf16[32,26624]{1,0:T(8,128)(2,1)} %reduce.5) | data formatting | bytes 3407872
  46.8 9.5 %all-to-all-start.1 = ((bf16[32,2,13312]{2,1,0:T(2,128)(2,1)}), bf16[32,2,13312]{2,1,0:T(2,128)(2,1)S(1)}, u32[]{:S(2)}, u32[]{:S(2)}) async-start(bf16[32,2,13312]{2,1,0:T(2,128)(2,1)} %reshape.436), calls=%async_computation.1 | async-start | bytes 3407872 | tf_op jit(solution)/shard_map/all_to_all | solution.py:121
  58.5 39.5 %all-to-all-done.1 = bf16[32,2,13312]{2,1,0:T(2,128)(2,1)S(1)} async-done(((bf16[32,2,13312]{2,1,0:T(2,128)(2,1)}), bf16[32,2,13312]{2,1,0:T(2,128)(2,1)S(1)}, u32[]{:S(2)}, u32[]{:S(2)}) %all-to-all-start.1) | async-done | bytes 1703968 | tf_op jit(solution)/shard_map/all_to_all | solution.py:121
  98.0 6.2 %reshape.437 = bf16[32,1,26624]{2,1,0:T(2,128)(2,1)} reshape(bf16[32,2,13312]{2,1,0:T(2,128)(2,1)S(1)} %all-to-all-done.1) | data formatting | bytes 3407872
  104.2 3.0 %copy.228 = bf16[32,1,26624]{2,0,1:T(8,128)(2,1)S(1)} copy(bf16[32,1,26624]{2,1,0:T(2,128)(2,1)} %reshape.437) | data formatting | bytes 3407872
  109.0 2.6 copy.170
  111.6 4.9 %slice_bitcast_fusion = (bf16[2048,32,2]{1,2,0:T(2,128)(2,1)}, bf16[2048,32,2]{1,2,0:T(2,128)(2,1)}) fusion(bf16[32,2048,4]{0,2,1:T(4,128)(2,1)} %bitcast.136), kind=kLoop, calls=%fused_computation.38 | loop fusion | bytes 1048576 | tf_op jit(solution)/shard_map/transpose | solution.py:136
  116.6 2.6 copy.176
  120.0 2.6 copy.171
  123.4 3.0 %reshape.345 = f32[32,256,64]{2,1,0:T(8,128)} reshape(f32[32,16384]{1,0:T(8,128)S(1)} %slice_convert_fusion) | data formatting | bytes 4194304 | tf_op jit(solution)/shard_map/convert_element_type | solution.py:137
  126.4 2.8 %multiply_reduce_fusion = f32[256]{0:T(256)S(1)} fusion(f32[32,256,64]{2,1,0:T(8,128)} %reshape.345), kind=kLoop, calls=%fused_computation.11 | loop fusion | flops 1048320 | bytes 2098176 | tf_op jit(solution)/shard_map/reduce_sum | solution.py:17
  129.8 2.1 fusion.1
  131.9 2.0 copy.169
  134.5 2.8 %copy.165 = f32[256,32,64]{0,2,1:T(8,128)S(1)} copy(f32[256,32,64]{2,0,1:T(8,128)} %bitcast.132) | data formatting | bytes 4194304 | tf_op jit(solution)/shard_map/convert_element_type | solution.py:137
  137.4 2.1 reshape.340
  139.5 6.9 %multiply_convert_fusion.1 = bf16[2,128,2048]{1,0,2:T(2,128)(2,1)S(1)} fusion(f32[2,128,2048]{1,0,2:T(2,128)} %reshape.340, f32[2048]{0:T(1024)S(1)} %copy-done.18, f32[2,128]{1,0:T(2,128)S(1)} %get-tuple-element.18), kind=kLoop, calls=%fused_computation.21 | loop fusion | flops 1572864 | bytes 3154944 | tf_op jit(solution)/shard_map/convert_element_type | solution.py:18
  149.5 4.2 %all-to-all-start.2 = ((bf16[32,256,64]{1,2,0:T(8,128)(2,1)}), bf16[32,256,64]{1,2,0:T(8,128)(2,1)S(1)}, u32[]{:S(2)}, u32[]{:S(2)}) async-start(bf16[32,256,64]{1,2,0:T(8,128)(2,1)} %bitcast.19), calls=%async_computation.2 | async-start | bytes 2097152 | tf_op jit(solution)/shard_map/all_to_all | solution.py:45
  153.9 27.7 %all-to-all-done.2 = bf16[32,256,64]{1,2,0:T(8,128)(2,1)S(1)} async-done(((bf16[32,256,64]{1,2,0:T(8,128)(2,1)}), bf16[32,256,64]{1,2,0:T(8,128)(2,1)S(1)}, u32[]{:S(2)}, u32[]{:S(2)}) %all-to-all-start.2) | async-done | bytes 1048608 | tf_op jit(solution)/shard_map/all_to_all | solution.py:45
  182.9 3.9 %all-to-all-start.3 = ((bf16[32,256,64]{1,2,0:T(8,128)(2,1)}), bf16[32,256,64]{1,2,0:T(8,128)(2,1)S(1)}, u32[]{:S(2)}, u32[]{:S(2)}) async-start(bf16[32,256,64]{1,2,0:T(8,128)(2,1)} %broadcast_in_dim.160), calls=%async_computation.3 | async-start | bytes 2097152 | tf_op jit(solution)/shard_map/all_to_all | solution.py:36
  186.8 27.8 %all-to-all-done.3 = bf16[32,256,64]{1,2,0:T(8,128)(2,1)S(1)} async-done(((bf16[32,256,64]{1,2,0:T(8,128)(2,1)}), bf16[32,256,64]{1,2,0:T(8,128)(2,1)S(1)}, u32[]{:S(2)}, u32[]{:S(2)}) %all-to-all-start.3) | async-done | bytes 1048608 | tf_op jit(solution)/shard_map/all_to_all | solution.py:36
  215.3 2.4 fusion.45
  217.7 2.6 convolution_convert_fusion
  221.6 4.0 %all-to-all-start.4 = ((bf16[32,256,64]{1,2,0:T(8,128)(2,1)}), bf16[32,256,64]{1,2,0:T(8,128)(2,1)S(1)}, u32[]{:S(2)}, u32[]{:S(2)}) async-start(bf16[32,256,64]{1,2,0:T(8,128)(2,1)} %bitcast.24), calls=%async_computation.4 | async-start | bytes 2097152 | tf_op jit(solution)/shard_map/all_to_all | solution.py:45
  225.7 27.8 %all-to-all-done.4 = bf16[32,256,64]{1,2,0:T(8,128)(2,1)S(1)} async-done(((bf16[32,256,64]{1,2,0:T(8,128)(2,1)}), bf16[32,256,64]{1,2,0:T(8,128)(2,1)S(1)}, u32[]{:S(2)}, u32[]{:S(2)}) %all-to-all-start.4) | async-done | bytes 1048608 | tf_op jit(solution)/shard_map/all_to_all | solution.py:45
  254.6 6.4 %all-to-all-start.5 = ((bf16[16,2,512]{2,1,0:T(2,128)(2,1)}), bf16[16,2,512]{2,1,0:T(2,128)(2,1)S(1)}, u32[]{:S(2)}, u32[]{:S(2)}) async-start(bf16[16,2,512]{2,1,0:T(2,128)(2,1)} %reshape.438), calls=%async_computation.5 | async-start | bytes 65536 | tf_op jit(solution)/shard_map/all_to_all | solution.py:193
  261.6 10.6 %all-to-all-done.5 = bf16[16,2,512]{2,1,0:T(2,128)(2,1)S(1)} async-done(((bf16[16,2,512]{2,1,0:T(2,128)(2,1)}), bf16[16,2,512]{2,1,0:T(2,128)(2,1)S(1)}, u32[]{:S(2)}, u32[]{:S(2)}) %all-to-all-start.5) | async-done | bytes 32800 | tf_op jit(solution)/shard_map/all_to_all | solution.py:193
  272.4 1.5 scatter_fusion
  (153 shorter events, 29.8 us)
Async XLA Ops:
  0.6 217.1 %copy-start = (bf16[256,2048]{1,0:T(8,128)(2,1)S(1)}, bf16[256,2048]{1,0:T(8,128)(2,1)}, u32[]{:S(2)}) copy-start(bf16[256,2048]{1,0:T(8,128)(2,1)} %param.33) | copy-start | bytes 3145732
  0.6 24.5 %copy-start.27 = (s32[128]{0:T(128)S(1)}, s32[128]{0:T(128)}, u32[]{:S(2)}) copy-start(s32[128]{0:T(128)} %constant.166) | copy-start | bytes 1540
  0.7 22.5 %copy-start.1 = (s32[32]{0:T(128)S(1)}, s32[32]{0:T(128)}, u32[]{:S(2)}) copy-start(s32[32]{0:T(128)} %param.23) | copy-start | bytes 388
  0.7 23.1 %copy-start.2 = (s32[32,1]{0,1:T(1,128)S(1)}, s32[32,1]{0,1:T(1,128)}, u32[]{:S(2)}) copy-start(s32[32,1]{0,1:T(1,128)} %param.21) | copy-start | bytes 388
  0.7 23.8 %copy-start.3 = (s32[32]{0:T(128)S(1)}, s32[32]{0:T(128)}, u32[]{:S(2)}) copy-start(s32[32]{0:T(128)} %param.20) | copy-start | bytes 388
  0.7 24.4 %copy-start.16 = (bf16[2048,16]{0,1:T(8,128)(2,1)S(1)}, bf16[2048,16]{0,1:T(8,128)(2,1)}, u32[]{:S(2)}) copy-start(bf16[2048,16]{0,1:T(8,128)(2,1)} %param.28) | copy-start | bytes 196612
  0.7 24.4 %copy-start.17 = (bf16[2048,16]{0,1:T(8,128)(2,1)S(1)}, bf16[2048,16]{0,1:T(8,128)(2,1)}, u32[]{:S(2)}) copy-start(bf16[2048,16]{0,1:T(8,128)(2,1)} %param.27) | copy-start | bytes 196612
  6.9 29.8 %all-to-all-start = ((bf16[16,2,4608]{2,1,0:T(2,128)(2,1)}), bf16[16,2,4608]{2,1,0:T(2,128)(2,1)}, u32[]{:S(2)}, u32[]{:S(2)}) async-start(bf16[16,2,4608]{2,1,0:T(2,128)(2,1)} %reshape.434), calls=%async_computation | async-start | bytes 589824 | tf_op jit(solution)/shard_map/all_to_all | solution.py:96
  27.1 4.7 %copy-start.4 = (s32[16]{0:T(128)S(1)}, s32[16]{0:T(128)}, u32[]{:S(2)}) copy-start(s32[16]{0:T(128)} %param.22) | copy-start | bytes 196
  30.2 2.2 copy-start.26
  32.4 8.3 %copy-start.6 = (bf16[32,8192]{1,0:T(8,128)(2,1)S(1)}, bf16[32,8192]{1,0:T(8,128)(2,1)}, u32[]{:S(2)}) copy-start(bf16[32,8192]{1,0:T(8,128)(2,1)} %copy.163) | copy-start | bytes 1572868
  46.8 9.5 %copy-start.20 = (bf16[2048]{0:T(1024)(128)(2,1)S(1)}, bf16[2048]{0:T(1024)(128)(2,1)}, u32[]{:S(2)}) copy-start(bf16[2048]{0:T(1024)(128)(2,1)} %param.25) | copy-start | bytes 12292
  46.8 51.1 %all-to-all-start.1 = ((bf16[32,2,13312]{2,1,0:T(2,128)(2,1)}), bf16[32,2,13312]{2,1,0:T(2,128)(2,1)S(1)}, u32[]{:S(2)}, u32[]{:S(2)}) async-start(bf16[32,2,13312]{2,1,0:T(2,128)(2,1)} %reshape.436), calls=%async_computation.1 | async-start | bytes 3407872 | tf_op jit(solution)/shard_map/all_to_all | solution.py:121
  57.1 47.1 %copy-start.21 = (pred[2,128]{1,0:T(4,128)(4,1)}, pred[2,128]{1,0:T(4,128)(4,1)S(1)}, u32[]{:S(2)}) copy-start(pred[2,128]{1,0:T(4,128)(4,1)S(1)} %iota_compare_fusion.1) | copy-start | bytes 772
  126.4 3.4 %copy-start.5 = (f32[32,256,64]{2,1,0:T(8,128)S(1)}, f32[32,256,64]{2,1,0:T(8,128)}, u32[]{:S(2)}) copy-start(f32[32,256,64]{2,1,0:T(8,128)} %reshape.345) | copy-start | bytes 6291460
  131.9 2.0 copy-start.7
  131.9 2.3 copy-start.8
  137.4 2.1 copy-start.18
  139.5 7.0 %copy-start.28 = (bf16[2048,64]{0,1:T(8,128)(2,1)S(1)}, bf16[2048,64]{0,1:T(8,128)(2,1)}, u32[]{:S(2)}) copy-start(bf16[2048,64]{0,1:T(8,128)(2,1)} %param.26) | copy-start | bytes 786436
  139.5 7.3 %copy-start.13 = (f32[128,32]{0,1:T(8,128)S(1)}, f32[128,32]{0,1:T(8,128)}, u32[]{:S(2)}) copy-start(f32[128,32]{0,1:T(8,128)} %get-tuple-element.20) | copy-start | bytes 49156
  139.5 7.3 %copy-start.14 = (f32[128,32]{0,1:T(8,128)S(1)}, f32[128,32]{0,1:T(8,128)}, u32[]{:S(2)}) copy-start(f32[128,32]{0,1:T(8,128)} %get-tuple-element.21) | copy-start | bytes 49156
  139.5 7.8 %copy-start.19 = (pred[2,128,128]{2,1,0:T(8,128)(4,1)S(1)}, pred[2,128,128]{2,1,0:T(8,128)(4,1)}, u32[]{:S(2)}) copy-start(pred[2,128,128]{2,1,0:T(8,128)(4,1)} %broadcast_and_fusion) | copy-start | bytes 98308
  146.4 1.1 copy-start.15
  146.5 1.3 copy-start.12
  148.2 5.5 %copy-start.10 = (bf16[16,2,8,64]{3,2,1,0:T(8,128)(2,1)S(1)}, bf16[16,2,8,64]{3,2,1,0:T(8,128)(2,1)}, u32[]{:S(2)}) copy-start(bf16[16,2,8,64]{3,2,1,0:T(8,128)(2,1)} %copy-done.9) | copy-start | bytes 98308
  149.5 32.0 %all-to-all-start.2 = ((bf16[32,256,64]{1,2,0:T(8,128)(2,1)}), bf16[32,256,64]{1,2,0:T(8,128)(2,1)S(1)}, u32[]{:S(2)}, u32[]{:S(2)}) async-start(bf16[32,256,64]{1,2,0:T(8,128)(2,1)} %bitcast.19), calls=%async_computation.2 | async-start | bytes 2097152 | tf_op jit(solution)/shard_map/all_to_all | solution.py:45
  153.9 33.0 %copy-start.23 = (bf16[2048]{0:T(1024)(128)(2,1)S(1)}, bf16[2048]{0:T(1024)(128)(2,1)}, u32[]{:S(2)}) copy-start(bf16[2048]{0:T(1024)(128)(2,1)} %param.30) | copy-start | bytes 12292
  182.9 31.8 %all-to-all-start.3 = ((bf16[32,256,64]{1,2,0:T(8,128)(2,1)}), bf16[32,256,64]{1,2,0:T(8,128)(2,1)S(1)}, u32[]{:S(2)}, u32[]{:S(2)}) async-start(bf16[32,256,64]{1,2,0:T(8,128)(2,1)} %broadcast_in_dim.160), calls=%async_computation.3 | async-start | bytes 2097152 | tf_op jit(solution)/shard_map/all_to_all | solution.py:36
  221.6 32.1 %copy-start.22 = (pred[2,128]{1,0:T(4,128)(4,1)S(1)}, pred[2,128]{1,0:T(4,128)(4,1)}, u32[]{:S(2)}) copy-start(pred[2,128]{1,0:T(4,128)(4,1)} %copy-done.21) | copy-start | bytes 772
  221.6 50.7 %copy-start.25 = (s32[32]{0:T(128)S(1)}, s32[32]{0:T(128)}, u32[]{:S(2)}) copy-start(s32[32]{0:T(128)} %copy-done.24) | copy-start | bytes 388
  221.6 31.9 %all-to-all-start.4 = ((bf16[32,256,64]{1,2,0:T(8,128)(2,1)}), bf16[32,256,64]{1,2,0:T(8,128)(2,1)S(1)}, u32[]{:S(2)}, u32[]{:S(2)}) async-start(bf16[32,256,64]{1,2,0:T(8,128)(2,1)} %bitcast.24), calls=%async_computation.4 | async-start | bytes 2097152 | tf_op jit(solution)/shard_map/all_to_all | solution.py:45
  254.6 17.6 %all-to-all-start.5 = ((bf16[16,2,512]{2,1,0:T(2,128)(2,1)}), bf16[16,2,512]{2,1,0:T(2,128)(2,1)S(1)}, u32[]{:S(2)}, u32[]{:S(2)}) async-start(bf16[16,2,512]{2,1,0:T(2,128)(2,1)} %reshape.438), calls=%async_computation.5 | async-start | bytes 65536 | tf_op jit(solution)/shard_map/all_to_all | solution.py:193
  (3 other events, 2.1 us)
where the time goes:
time: 276 us; the launch traced here: 275 us
  waiting for transfers between devices  138 us (50%)
  local copies, waits for them, and re-layouts  62.9 us (23%)
  starting transfers between devices  44.2 us (16%)
  other arithmetic  21.3 us (8%)
  matrix products  6.94 us (3%)
    all_to_all x2, waiting for transfers between devices, scatter_sum(): got = lax.all_to_all(sent, axis_name, 0, 0, tiled=True)  55.5 us
    all_to_all x1, waiting for transfers between devices, shards(): lax.all_to_all(jnp.concatenate([state_sent, prefix_sent, w_sent], axis=1)...  39.5 us
    all_to_all x1, waiting for transfers between devices, gather_rows(): got = lax.all_to_all(sent, axis_name, 0, 0, tiled=True)  27.8 us
    unnamed x73, local copies, waits for them, and re-layouts  19.6 us
    all_to_all x1, starting transfers between devices, shards(): lax.all_to_all(jnp.concatenate([state_part, prefix_part], axis=1), 'dp',...  16.2 us
    all_to_all x1, waiting for transfers between devices, shards(): lax.all_to_all(result, 'dp', split_axis=1, concat_axis=0, tiled=True)  10.6 us
    all_to_all x1, starting transfers between devices, shards(): lax.all_to_all(jnp.concatenate([state_sent, prefix_sent, w_sent], axis=1)...  9.49 us
    all_to_all x2, starting transfers between devices, scatter_sum(): got = lax.all_to_all(sent, axis_name, 0, 0, tiled=True)  8.18 us
  transfers between devices with their start and end apart: 6, of which 6 were waited for; matrix products, arithmetic and copies ran while one was open for 4% of the time, Pallas kernels for 0%

commit v1 on v0

--- a/solution.py
+++ b/solution.py
@@ -1,8 +1,10 @@
+import functools
 import jax
 import jax.numpy as jnp
 import numpy as np
 from jax import lax
 from jax.sharding import PartitionSpec as P
+from jax.lax import all_to_all, axis_size
 
 H = 32
 KVH = 8
@@ -11,6 +13,18 @@
 P_SIZE = 256
 THETA = 10000000.0
 EPSILON = 1e-05
+
+
+def detail_the_regions(xin, peer_axis):
+    local_now = axis_size(peer_axis)
+    z = jnp.split(xin, local_now, axis=1)
+    p_next = jnp.stack(z, 0)
+    carry = all_to_all(p_next, axis_name=peer_axis, split_axis=0, concat_axis=0)
+    low = jnp.concatenate(carry, 0)
+    return low
+
+
+_lay_row = functools.partial(detail_the_regions, peer_axis="dp")
 
 
 def rms_scale(wide, gain):
@@ -190,7 +204,7 @@
         .astype(jnp.bfloat16)
         .reshape(local_reqs, L_MAX, width_here)
     )
-    returned = lax.all_to_all(result, "dp", split_axis=1, concat_axis=0, tiled=True)
+    returned = _lay_row(result)
     hidden_out = jnp.zeros_like(returned).at[request_order].set(returned)
     return (hidden_out, keys_out, values_out)
 

time: 276 us -> 278 us (level)
    unnamed x73 -> x90, local copies, waits for them, and re-layouts: 19.6 us -> 19 us
where the time goes in v1:
time: 278 us; the launch traced here: 276 us
  waiting for transfers between devices  140 us (50%)
  local copies, waits for them, and re-layouts  64.9 us (23%)
  starting transfers between devices  42.1 us (15%)
  other arithmetic  22.1 us (8%)
  matrix products  6.2 us (2%)
    all_to_all x2, waiting for transfers between devices, scatter_sum(): got = lax.all_to_all(sent, axis_name, 0, 0, tiled=True)  55.5 us
    all_to_all x1, waiting for transfers between devices, shards(): lax.all_to_all(jnp.concatenate([state_sent, prefix_sent, w_sent], axis=1)...  39.5 us
    all_to_all x1, waiting for transfers between devices, gather_rows(): got = lax.all_to_all(sent, axis_name, 0, 0, tiled=True)  27.8 us
    unnamed x90, local copies, waits for them, and re-layouts  19 us
    all_to_all x1, starting transfers between devices, shards(): lax.all_to_all(jnp.concatenate([state_part, prefix_part], axis=1), 'dp',...  16.2 us
    all_to_all x1, waiting for transfers between devices, detail_the_regions(): carry = all_to_all(p_next, axis_name=peer_axis, split_axis=0, concat_axis=0)  9.92 us
    all_to_all x1, starting transfers between devices, shards(): lax.all_to_all(jnp.concatenate([state_sent, prefix_sent, w_sent], axis=1)...  9.49 us
    all_to_all x2, starting transfers between devices, scatter_sum(): got = lax.all_to_all(sent, axis_name, 0, 0, tiled=True)  8.18 us
  transfers between devices with their start and end apart: 6, of which 6 were waited for; matrix products, arithmetic and copies ran while one was open for 4% of the time, Pallas kernels for 0%

profile of v1, /device:TPU:1, one launch (start us, length us, event | category | flops | bytes accessed | tf_op | source)
XLA Modules:
  0.0 276.4 jit_solution(17467148382611286234)
XLA Ops:
  10.6 16.2 %all-to-all-start = ((bf16[16,2,4608]{2,1,0:T(2,128)(2,1)}), bf16[16,2,4608]{2,1,0:T(2,128)(2,1)}, u32[]{:S(2)}, u32[]{:S(2)}) async-start(bf16[16,2,4608]{2,1,0:T(2,128)(2,1)} %reshape.438), calls=%async_computation | async-start | bytes 589824 | tf_op jit(solution)/shard_map/all_to_all | solution.py:110
  28.9 3.1 %copy.97 = bf16[2048,32,4]{1,2,0:T(4,128)(2,1)S(1)} copy(bf16[2048,32,4]{0,2,1:T(4,128)(2,1)} %gather.30) | data formatting | bytes 1048576 | tf_op jit(solution)/shard_map/jit(_take)/gather | solution.py:100
  33.5 6.9 %all-to-all-done = bf16[16,2,4608]{2,1,0:T(2,128)(2,1)} async-done(((bf16[16,2,4608]{2,1,0:T(2,128)(2,1)}), bf16[16,2,4608]{2,1,0:T(2,128)(2,1)}, u32[]{:S(2)}, u32[]{:S(2)}) %all-to-all-start) | async-done | bytes 294944 | tf_op jit(solution)/shard_map/all_to_all | solution.py:110
  40.4 2.2 reshape.439
  44.6 2.6 reduce.5
  47.2 3.3 %reshape.440 = bf16[32,2,13312]{2,1,0:T(2,128)(2,1)} reshape(bf16[32,26624]{1,0:T(8,128)(2,1)} %reduce.5) | data formatting | bytes 3407872
  50.6 9.5 %all-to-all-start.1 = ((bf16[32,2,13312]{2,1,0:T(2,128)(2,1)}), bf16[32,2,13312]{2,1,0:T(2,128)(2,1)S(1)}, u32[]{:S(2)}, u32[]{:S(2)}) async-start(bf16[32,2,13312]{2,1,0:T(2,128)(2,1)} %reshape.440), calls=%async_computation.1 | async-start | bytes 3407872 | tf_op jit(solution)/shard_map/all_to_all | solution.py:135
  62.2 39.5 %all-to-all-done.1 = bf16[32,2,13312]{2,1,0:T(2,128)(2,1)S(1)} async-done(((bf16[32,2,13312]{2,1,0:T(2,128)(2,1)}), bf16[32,2,13312]{2,1,0:T(2,128)(2,1)S(1)}, u32[]{:S(2)}, u32[]{:S(2)}) %all-to-all-start.1) | async-done | bytes 1703968 | tf_op jit(solution)/shard_map/all_to_all | solution.py:135
  101.7 6.2 %reshape.441 = bf16[32,1,26624]{2,1,0:T(2,128)(2,1)} reshape(bf16[32,2,13312]{2,1,0:T(2,128)(2,1)S(1)} %all-to-all-done.1) | data formatting | bytes 3407872
  108.0 3.0 %copy.153 = bf16[32,1,26624]{2,0,1:T(8,128)(2,1)S(1)} copy(bf16[32,1,26624]{2,1,0:T(2,128)(2,1)} %reshape.441) | data formatting | bytes 3407872
  112.8 2.6 copy.105
  115.4 5.0 %slice_bitcast_fusion = (bf16[2048,32,2]{1,2,0:T(2,128)(2,1)}, bf16[2048,32,2]{1,2,0:T(2,128)(2,1)}) fusion(bf16[32,2048,4]{0,2,1:T(4,128)(2,1)} %bitcast.181), kind=kLoop, calls=%fused_computation.38 | loop fusion | bytes 1048576 | tf_op jit(solution)/shard_map/transpose | solution.py:150
  120.4 2.6 copy.111
  123.8 2.6 copy.106
  127.2 3.0 %reshape.349 = f32[32,256,64]{2,1,0:T(8,128)} reshape(f32[32,16384]{1,0:T(8,128)S(1)} %slice_convert_fusion) | data formatting | bytes 4194304 | tf_op jit(solution)/shard_map/convert_element_type | solution.py:151
  130.2 2.8 %multiply_reduce_fusion = f32[256]{0:T(256)S(1)} fusion(f32[32,256,64]{2,1,0:T(8,128)} %reshape.349), kind=kLoop, calls=%fused_computation.11 | loop fusion | flops 1048320 | bytes 2098176 | tf_op jit(solution)/shard_map/reduce_sum | solution.py:31
  133.6 2.1 fusion.1
  135.7 2.0 copy.104
  138.9 2.8 %copy.100 = f32[256,32,64]{0,2,1:T(8,128)S(1)} copy(f32[256,32,64]{2,0,1:T(8,128)} %bitcast.177) | data formatting | bytes 4194304 | tf_op jit(solution)/shard_map/convert_element_type | solution.py:151
  141.8 2.1 reshape.344
  143.9 6.9 %multiply_convert_fusion.1 = bf16[2,128,2048]{1,0,2:T(2,128)(2,1)S(1)} fusion(f32[2,128,2048]{1,0,2:T(2,128)} %reshape.344, f32[2048]{0:T(1024)S(1)} %copy-done.18, f32[2,128]{1,0:T(2,128)S(1)} %get-tuple-element.16), kind=kLoop, calls=%fused_computation.21 | loop fusion | flops 1572864 | bytes 3154944 | tf_op jit(solution)/shard_map/convert_element_type | solution.py:32
  154.0 4.2 %all-to-all-start.2 = ((bf16[32,256,64]{1,2,0:T(8,128)(2,1)}), bf16[32,256,64]{1,2,0:T(8,128)(2,1)S(1)}, u32[]{:S(2)}, u32[]{:S(2)}) async-start(bf16[32,256,64]{1,2,0:T(8,128)(2,1)} %bitcast.19), calls=%async_computation.2 | async-start | bytes 2097152 | tf_op jit(solution)/shard_map/all_to_all | solution.py:59
  158.3 27.7 %all-to-all-done.2 = bf16[32,256,64]{1,2,0:T(8,128)(2,1)S(1)} async-done(((bf16[32,256,64]{1,2,0:T(8,128)(2,1)}), bf16[32,256,64]{1,2,0:T(8,128)(2,1)S(1)}, u32[]{:S(2)}, u32[]{:S(2)}) %all-to-all-start.2) | async-done | bytes 1048608 | tf_op jit(solution)/shard_map/all_to_all | solution.py:59
  187.3 3.9 %all-to-all-start.3 = ((bf16[32,256,64]{1,2,0:T(8,128)(2,1)}), bf16[32,256,64]{1,2,0:T(8,128)(2,1)S(1)}, u32[]{:S(2)}, u32[]{:S(2)}) async-start(bf16[32,256,64]{1,2,0:T(8,128)(2,1)} %broadcast_in_dim.160), calls=%async_computation.3 | async-start | bytes 2097152 | tf_op jit(solution)/shard_map/all_to_all | solution.py:50
  191.3 27.8 %all-to-all-done.3 = bf16[32,256,64]{1,2,0:T(8,128)(2,1)S(1)} async-done(((bf16[32,256,64]{1,2,0:T(8,128)(2,1)}), bf16[32,256,64]{1,2,0:T(8,128)(2,1)S(1)}, u32[]{:S(2)}, u32[]{:S(2)}) %all-to-all-start.3) | async-done | bytes 1048608 | tf_op jit(solution)/shard_map/all_to_all | solution.py:50
  219.8 1.7 fusion.43
  221.5 2.5 convolution_convert_fusion
  225.4 4.0 %all-to-all-start.4 = ((bf16[32,256,64]{1,2,0:T(8,128)(2,1)}), bf16[32,256,64]{1,2,0:T(8,128)(2,1)S(1)}, u32[]{:S(2)}, u32[]{:S(2)}) async-start(bf16[32,256,64]{1,2,0:T(8,128)(2,1)} %bitcast.25), calls=%async_computation.4 | async-start | bytes 2097152 | tf_op jit(solution)/shard_map/all_to_all | solution.py:59
  229.5 27.8 %all-to-all-done.4 = bf16[32,256,64]{1,2,0:T(8,128)(2,1)S(1)} async-done(((bf16[32,256,64]{1,2,0:T(8,128)(2,1)}), bf16[32,256,64]{1,2,0:T(8,128)(2,1)S(1)}, u32[]{:S(2)}, u32[]{:S(2)}) %all-to-all-start.4) | async-done | bytes 1048608 | tf_op jit(solution)/shard_map/all_to_all | solution.py:59
  258.6 4.3 %all-to-all-start.5 = ((bf16[16,2,512]{2,1,0:T(2,128)(2,1)}), bf16[16,2,512]{2,1,0:T(2,128)(2,1)S(1)}, u32[]{:S(2)}, u32[]{:S(2)}) async-start(bf16[16,2,512]{2,1,0:T(2,128)(2,1)} %reshape.442), calls=%async_computation.5 | async-start | bytes 65536 | tf_op jit(solution)/shard_map/all_to_all | solution.py:22
  264.2 9.9 %all-to-all-done.5 = bf16[16,2,512]{2,1,0:T(2,128)(2,1)S(1)} async-done(((bf16[16,2,512]{2,1,0:T(2,128)(2,1)}), bf16[16,2,512]{2,1,0:T(2,128)(2,1)S(1)}, u32[]{:S(2)}, u32[]{:S(2)}) %all-to-all-start.5) | async-done | bytes 32800 | tf_op jit(solution)/shard_map/all_to_all | solution.py:22
  274.3 1.5 scatter_fusion
  (168 shorter events, 32.4 us)
Async XLA Ops:
  0.6 220.8 %copy-start = (bf16[256,2048]{1,0:T(8,128)(2,1)S(1)}, bf16[256,2048]{1,0:T(8,128)(2,1)}, u32[]{:S(2)}) copy-start(bf16[256,2048]{1,0:T(8,128)(2,1)} %param.33) | copy-start | bytes 3145732
  0.6 6.8 %copy-start.21 = (bf16[1,8,1024]{2,1,0:T(8,128)(2,1)S(1)}, bf16[1,8,1024]{2,1,0:T(8,128)(2,1)}, u32[]{:S(2)}) copy-start(bf16[1,8,1024]{2,1,0:T(8,128)(2,1)} %param.24) | copy-start | bytes 49156
  0.7 6.8 %copy-start.14 = (bf16[32,8,64]{2,1,0:T(8,128)(2,1)S(1)}, bf16[32,8,64]{2,1,0:T(8,128)(2,1)}, u32[]{:S(2)}) copy-start(bf16[32,8,64]{2,1,0:T(8,128)(2,1)} %param.19) | copy-start | bytes 98308
  1.4 6.0 %copy-start.25 = (s32[32]{0:T(128)}, s32[32]{0:T(128)S(1)}, u32[]{:S(2)}) copy-start(s32[32]{0:T(128)S(1)} %compare_select_fusion.4) | copy-start | bytes 388
  3.4 23.5 %copy-start.27 = (s32[128]{0:T(128)S(1)}, s32[128]{0:T(128)}, u32[]{:S(2)}) copy-start(s32[128]{0:T(128)} %constant.166) | copy-start | bytes 1540
  3.4 23.5 %copy-start.28 = (s32[32]{0:T(128)S(1)}, s32[32]{0:T(128)}, u32[]{:S(2)}) copy-start(s32[32]{0:T(128)} %constant.165) | copy-start | bytes 388
  3.4 23.5 %copy-start.15 = (bf16[2048,16]{0,1:T(8,128)(2,1)S(1)}, bf16[2048,16]{0,1:T(8,128)(2,1)}, u32[]{:S(2)}) copy-start(bf16[2048,16]{0,1:T(8,128)(2,1)} %param.28) | copy-start | bytes 196612
  3.4 23.5 %copy-start.16 = (bf16[2048,16]{0,1:T(8,128)(2,1)S(1)}, bf16[2048,16]{0,1:T(8,128)(2,1)}, u32[]{:S(2)}) copy-start(bf16[2048,16]{0,1:T(8,128)(2,1)} %param.27) | copy-start | bytes 196612
  10.6 29.8 %all-to-all-start = ((bf16[16,2,4608]{2,1,0:T(2,128)(2,1)}), bf16[16,2,4608]{2,1,0:T(2,128)(2,1)}, u32[]{:S(2)}, u32[]{:S(2)}) async-start(bf16[16,2,4608]{2,1,0:T(2,128)(2,1)} %reshape.438), calls=%async_computation | async-start | bytes 589824 | tf_op jit(solution)/shard_map/all_to_all | solution.py:110
  33.5 10.9 %copy-start.2 = (bf16[32,8192]{1,0:T(8,128)(2,1)S(1)}, bf16[32,8192]{1,0:T(8,128)(2,1)}, u32[]{:S(2)}) copy-start(bf16[32,8192]{1,0:T(8,128)(2,1)} %copy.98) | copy-start | bytes 1572868
  50.6 9.5 %copy-start.20 = (bf16[2048]{0:T(1024)(128)(2,1)S(1)}, bf16[2048]{0:T(1024)(128)(2,1)}, u32[]{:S(2)}) copy-start(bf16[2048]{0:T(1024)(128)(2,1)} %param.25) | copy-start | bytes 12292
  50.6 51.1 %all-to-all-start.1 = ((bf16[32,2,13312]{2,1,0:T(2,128)(2,1)}), bf16[32,2,13312]{2,1,0:T(2,128)(2,1)S(1)}, u32[]{:S(2)}, u32[]{:S(2)}) async-start(bf16[32,2,13312]{2,1,0:T(2,128)(2,1)} %reshape.440), calls=%async_computation.1 | async-start | bytes 3407872 | tf_op jit(solution)/shard_map/all_to_all | solution.py:135
  60.9 47.1 %copy-start.22 = (pred[2,128]{1,0:T(4,128)(4,1)}, pred[2,128]{1,0:T(4,128)(4,1)S(1)}, u32[]{:S(2)}) copy-start(pred[2,128]{1,0:T(4,128)(4,1)S(1)} %iota_compare_fusion.1) | copy-start | bytes 772
  130.2 3.4 %copy-start.1 = (f32[32,256,64]{2,1,0:T(8,128)S(1)}, f32[32,256,64]{2,1,0:T(8,128)}, u32[]{:S(2)}) copy-start(f32[32,256,64]{2,1,0:T(8,128)} %reshape.349) | copy-start | bytes 6291460
  135.7 2.0 copy-start.5
  135.7 2.3 copy-start.6
  141.8 2.1 copy-start.18
  143.8 7.0 %copy-start.29 = (bf16[2048,64]{0,1:T(8,128)(2,1)S(1)}, bf16[2048,64]{0,1:T(8,128)(2,1)}, u32[]{:S(2)}) copy-start(bf16[2048,64]{0,1:T(8,128)(2,1)} %param.26) | copy-start | bytes 786436
  143.9 7.3 %copy-start.11 = (f32[128,32]{0,1:T(8,128)S(1)}, f32[128,32]{0,1:T(8,128)}, u32[]{:S(2)}) copy-start(f32[128,32]{0,1:T(8,128)} %get-tuple-element.18) | copy-start | bytes 49156
  143.9 7.3 %copy-start.12 = (f32[128,32]{0,1:T(8,128)S(1)}, f32[128,32]{0,1:T(8,128)}, u32[]{:S(2)}) copy-start(f32[128,32]{0,1:T(8,128)} %get-tuple-element.19) | copy-start | bytes 49156
  143.9 7.8 %copy-start.19 = (pred[2,128,128]{2,1,0:T(8,128)(4,1)S(1)}, pred[2,128,128]{2,1,0:T(8,128)(4,1)}, u32[]{:S(2)}) copy-start(pred[2,128,128]{2,1,0:T(8,128)(4,1)} %broadcast_and_fusion) | copy-start | bytes 98308
  150.9 1.3 copy-start.8
  151.2 2.7 copy-start.9
  152.6 5.5 %copy-start.4 = (bf16[16,2,8,64]{3,2,1,0:T(8,128)(2,1)S(1)}, bf16[16,2,8,64]{3,2,1,0:T(8,128)(2,1)}, u32[]{:S(2)}) copy-start(bf16[16,2,8,64]{3,2,1,0:T(8,128)(2,1)} %copy-done.3) | copy-start | bytes 98308
  154.0 32.0 %all-to-all-start.2 = ((bf16[32,256,64]{1,2,0:T(8,128)(2,1)}), bf16[32,256,64]{1,2,0:T(8,128)(2,1)S(1)}, u32[]{:S(2)}, u32[]{:S(2)}) async-start(bf16[32,256,64]{1,2,0:T(8,128)(2,1)} %bitcast.19), calls=%async_computation.2 | async-start | bytes 2097152 | tf_op jit(solution)/shard_map/all_to_all | solution.py:59
  158.3 33.0 %copy-start.24 = (bf16[2048]{0:T(1024)(128)(2,1)S(1)}, bf16[2048]{0:T(1024)(128)(2,1)}, u32[]{:S(2)}) copy-start(bf16[2048]{0:T(1024)(128)(2,1)} %param.30) | copy-start | bytes 12292
  187.3 31.8 %all-to-all-start.3 = ((bf16[32,256,64]{1,2,0:T(8,128)(2,1)}), bf16[32,256,64]{1,2,0:T(8,128)(2,1)S(1)}, u32[]{:S(2)}, u32[]{:S(2)}) async-start(bf16[32,256,64]{1,2,0:T(8,128)(2,1)} %broadcast_in_dim.160), calls=%async_computation.3 | async-start | bytes 2097152 | tf_op jit(solution)/shard_map/all_to_all | solution.py:50
  225.3 32.2 %copy-start.23 = (pred[2,128]{1,0:T(4,128)(4,1)S(1)}, pred[2,128]{1,0:T(4,128)(4,1)}, u32[]{:S(2)}) copy-start(pred[2,128]{1,0:T(4,128)(4,1)} %copy-done.22) | copy-start | bytes 772
  225.3 37.5 %copy-start.10 = (bf16[2,128,32]{1,2,0:T(8,128)(2,1)S(1)}, bf16[2,128,32]{1,2,0:T(8,128)(2,1)}, u32[]{:S(2)}) copy-start(bf16[2,128,32]{1,2,0:T(8,128)(2,1)} %copy-done.9) | copy-start | bytes 49156
  225.4 48.9 %copy-start.26 = (s32[32]{0:T(128)S(1)}, s32[32]{0:T(128)}, u32[]{:S(2)}) copy-start(s32[32]{0:T(128)} %copy-done.25) | copy-start | bytes 388
  225.4 31.9 %all-to-all-start.4 = ((bf16[32,256,64]{1,2,0:T(8,128)(2,1)}), bf16[32,256,64]{1,2,0:T(8,128)(2,1)S(1)}, u32[]{:S(2)}, u32[]{:S(2)}) async-start(bf16[32,256,64]{1,2,0:T(8,128)(2,1)} %bitcast.25), calls=%async_computation.4 | async-start | bytes 2097152 | tf_op jit(solution)/shard_map/all_to_all | solution.py:59
  258.6 15.6 %all-to-all-start.5 = ((bf16[16,2,512]{2,1,0:T(2,128)(2,1)}), bf16[16,2,512]{2,1,0:T(2,128)(2,1)S(1)}, u32[]{:S(2)}, u32[]{:S(2)}) async-start(bf16[16,2,512]{2,1,0:T(2,128)(2,1)} %reshape.442), calls=%async_computation.5 | async-start | bytes 65536 | tf_op jit(solution)/shard_map/all_to_all | solution.py:22
  (4 other events, 3.7 us)
